TPU v7x, 32 devices: a whole 2x2x4 slice. The times are simulated.
32 devices in a mesh: dp: 8 (over z, core), tensor: 4 (over y, x).
Axes of the slice: x: 2, y: 2, z: 4, core: 2. Of those that a mesh axis runs over, the one named last changes fastest.
Arguments:
- tokens: bfloat16 [512, 8192], P(None, 'dp'), may hold values from -6 to 6
- w_gate_up: bfloat16 [8192, 2, 28672], P('dp', None, 'tensor'), may hold values from -0.0625 to 0.0625
- w_down: bfloat16 [28672, 8192], P('tensor', 'dp'), may hold values from -0.03125 to 0.03125
- targets: bfloat16 [512, 8192], P(None, 'dp'), may hold values from -3 to 3
- proj_model: bfloat16 [8192, 128], P('dp'), may hold values from -0.0625 to 0.0625
- proj_hidden: bfloat16 [28672, 192], P('tensor'), may hold values from -0.03125 to 0.03125
- store: bfloat16 [4096, 12288], P(('dp', 'tensor')), may hold values from -0.017944336 to 0.017944336
Outputs:
- scores: float32 [4, 4096], P(None, ('dp', 'tensor'))
All inputs are finite; a program needn't handle non-finite values.
Results may differ from a plain program's by a relative error of at most 0.02.
Values may be sent and summed in bfloat16 or wider, within the bound.
No kernel may reach another device: no remote copies, remote signals or barrier semaphores. Data moves between devices by JAX's collectives and lax.ppermute only.
A program may use at most 256 MiB of HBM per device.

v0:
```python
import jax
import jax.numpy as jnp
import numpy as np
from jax import lax
from jax.sharding import Mesh, PartitionSpec as P

RANK = 64
SEQ = 128


def local(tokens, w_gate_up, w_down, targets, proj_model, proj_hidden, store):
    n_z = lax.axis_size("z")
    n_core = lax.axis_size("core")
    n_t = lax.axis_size("tensor")
    z = lax.axis_index("z")
    core = lax.axis_index("core")
    t_idx = lax.axis_index("tensor")
    total = tokens.shape[0]
    rows_z = total // n_z
    rows_t = total // n_t
    width_ff = w_down.shape[0]
    width_h = width_ff // n_core
    hi = lax.Precision.HIGHEST
    tests = total // SEQ

    def over_dp(part):
        part = lax.psum_scatter(
            part.reshape(total, n_core, width_h), "core", scatter_dimension=1, tiled=False
        )
        part = lax.psum_scatter(part.astype(jnp.bfloat16), "z", scatter_dimension=0, tiled=True)
        return part.astype(jnp.float32)

    a_in_part = jnp.dot(tokens, proj_model[:, :RANK], preferred_element_type=jnp.float32)
    gate = over_dp(jnp.dot(tokens, w_gate_up[:, 0, :], preferred_element_type=jnp.float32))
    up = over_dp(jnp.dot(tokens, w_gate_up[:, 1, :], preferred_element_type=jnp.float32))
    sig = jax.nn.sigmoid(gate)
    act = gate * sig
    hidden_loc = (act * up).astype(jnp.bfloat16)
    hidden = lax.all_gather(hidden_loc, "z", axis=0, tiled=True)
    hidden = lax.all_gather(hidden, "core", axis=1, tiled=True)
    out_part = jnp.dot(hidden, w_down, preferred_element_type=jnp.float32)
    out_rows = lax.psum_scatter(out_part, "tensor", scatter_dimension=0, tiled=True)
    tgt_rows = lax.dynamic_slice_in_dim(targets, t_idx * rows_t, rows_t, 0)
    cot_rows = (out_rows - tgt_rows.astype(jnp.float32)).astype(jnp.bfloat16)
    cot = lax.all_gather(cot_rows, "tensor", axis=0, tiled=True)
    a_out_part = jnp.dot(cot, proj_model[:, RANK:], preferred_element_type=jnp.float32)
    side = lax.psum(jnp.concatenate([a_in_part, a_out_part], axis=1), ("z", "core"))
    dh = over_dp(
        lax.dot_general(cot, w_down, (((1,), (1,)), ((), ())), preferred_element_type=jnp.float32)
    )
    dgate = (dh * up * sig * (1.0 + gate * (1.0 - sig))).astype(jnp.bfloat16)
    dup = (dh * act).astype(jnp.bfloat16)
    ph = lax.dynamic_slice_in_dim(proj_hidden, core * width_h, width_h, 0)
    b_part = jnp.concatenate(
        [
            jnp.dot(dgate, ph[:, :RANK], preferred_element_type=jnp.float32),
            jnp.dot(dup, ph[:, RANK : 2 * RANK], preferred_element_type=jnp.float32),
            jnp.dot(hidden_loc, ph[:, 2 * RANK :], preferred_element_type=jnp.float32),
        ],
        axis=1,
    )
    b_sum = lax.psum(b_part, ("core", "tensor"))
    side_z = lax.dynamic_slice_in_dim(side, z * rows_z, rows_z, 0)
    a_in = side_z[:, :RANK]
    a_out = side_z[:, RANK:]
    position = z * rows_z + lax.iota(jnp.int32, rows_z)
    member = ((position // SEQ)[:, None] == lax.iota(jnp.int32, tests)[None, :]).astype(jnp.float32)
    g_gate = jnp.einsum("ts,ti,tj->sij", member, a_in, b_sum[:, :RANK], precision=hi)
    g_up = jnp.einsum("ts,ti,tj->sij", member, a_in, b_sum[:, RANK : 2 * RANK], precision=hi)
    g_down = jnp.einsum("ts,ti,tj->sij", member, b_sum[:, 2 * RANK :], a_out, precision=hi)
    grads = lax.psum(jnp.stack([g_gate, g_up, g_down], axis=1).reshape(tests, 3 * RANK * RANK), "z")
    return lax.dot_general(
        grads.astype(jnp.bfloat16),
        store,
        (((1,), (1,)), ((), ())),
        preferred_element_type=jnp.float32,
    )


def solution(mesh):
    n_dp = mesh.shape["dp"]
    n_t = mesh.shape["tensor"]
    devices = np.asarray(mesh.devices).reshape(n_dp // 2, 2, n_t)
    fine = Mesh(devices, ("z", "core", "tensor"))
    dp = ("z", "core")
    return jax.shard_map(
        local,
        mesh=fine,
        in_specs=(
            P(None, dp),
            P(dp, None, "tensor"),
            P("tensor", dp),
            P(None, dp),
            P(dp, None),
            P("tensor", None),
            P(dp + ("tensor",), None),
        ),
        out_specs=P(None, dp + ("tensor",)),
        check_vma=False,
    )
```

profile of v0, /device:TPU:0, one launch (start us, length us, event | category | flops | bytes accessed | tf_op | source)
XLA Modules:
  0.0 831.2 jit_solution(7446013001953596638)
XLA Ops:
  6.5 55.9 %fusion.40 = (bf16[1024,1,7168]{2,1,0:T(2,128)(2,1)}, bf16[1024,1,7168]{2,1,0:T(2,128)(2,1)}) fusion(bf16[1024,2,7168]{2,1,0:T(2,128)(2,1)} %param.8), kind=kLoop, calls=%fused_computation.63 | loop fusion | bytes 58720256 | tf_op jit(solution)/shard_map/slice | solution.py:34
  62.4 60.0 %copy.21 = bf16[1024,1,7168]{0,2,1:T(8,128)(2,1)} copy(bf16[1024,1,7168]{2,1,0:T(2,128)(2,1)} %get-tuple-element.6) | data formatting | bytes 29360128 | tf_op jit(solution)/shard_map/dot_general | solution.py:35
  122.4 14.3 %fusion.9 = f32[512,2,3584]{2,0,1:T(8,128)} fusion(bf16[2,3584,1024]{2,1,0:T(8,128)(2,1)} %bitcast.58, bf16[512,1024]{1,0:T(8,128)(2,1)} %param.7), kind=kOutput, calls=%fused_computation.21 | convolution fusion | flops 7516192768 | bytes 30408704 | tf_op jit(solution)/shard_map/dot_general | solution.py:35
  136.7 0.0 reduce-scatter.8.cloned.1.call-start
  136.8 61.2 %copy.20 = bf16[1024,1,7168]{0,2,1:T(8,128)(2,1)} copy(bf16[1024,1,7168]{2,1,0:T(2,128)(2,1)} %get-tuple-element.5) | data formatting | bytes 29360128 | tf_op jit(solution)/shard_map/dot_general | solution.py:34
  198.0 14.4 %fusion.11 = f32[512,2,3584]{2,0,1:T(8,128)} fusion(bf16[2,3584,1024]{2,1,0:T(8,128)(2,1)} %bitcast.59, bf16[512,1024]{1,0:T(8,128)(2,1)} %param.7), kind=kOutput, calls=%fused_computation.23 | convolution fusion | flops 7516192768 | bytes 30408704 | tf_op jit(solution)/shard_map/dot_general | solution.py:34
  212.4 5.4 convert_bitcast_fusion.1
  217.8 0.0 reduce-scatter.10.cloned.1.call-start
  217.9 21.3 %reduce-scatter.8.cloned.1.call-done = f32[512,1,3584]{2,0,1:T(8,128)} async-done(((f32[512,2,3584]{2,0,1:T(8,128)}), f32[512,1,3584]{2,0,1:T(8,128)}) %reduce-scatter.8.cloned.1.call-update) | async-done | bytes 7340048 | tf_op jit(solution)/shard_map/reduce_scatter | solution.py:27
  239.2 5.3 convert_bitcast_fusion.2
  244.5 0.0 all-gather.4.cloned.1.call-start
  244.6 66.6 %reduce-scatter.14.cloned.1.call-done = bf16[128,3584]{1,0:T(8,128)(2,1)} async-done(((bf16[512,3584]{1,0:T(8,128)(2,1)}), bf16[128,3584]{1,0:T(8,128)(2,1)}) %reduce-scatter.14.cloned.1.call-update) | async-done | bytes 917520 | tf_op jit(solution)/shard_map/reduce_scatter | solution.py:30
  311.1 71.0 %reduce-scatter.10.cloned.1.call-done = bf16[128,3584]{1,0:T(8,128)(2,1)} async-done(((bf16[512,3584]{1,0:T(8,128)(2,1)}), bf16[128,3584]{1,0:T(8,128)(2,1)}) %reduce-scatter.10.cloned.1.call-update) | async-done | bytes 917520 | tf_op jit(solution)/shard_map/reduce_scatter | solution.py:30
  382.1 2.9 fusion
  385.1 72.6 %all-gather.4.cloned.1.call-done = bf16[512,3584]{1,0:T(8,128)(2,1)} async-done(((bf16[128,3584]{1,0:T(8,128)(2,1)}), bf16[512,3584]{1,0:T(8,128)(2,1)}) %all-gather.4.cloned.1.call-update) | async-done | bytes 3670032 | tf_op jit(solution)/shard_map/all_gather | solution.py:39
  457.7 0.2 reduce-scatter.16.cloned.1.call-start
  458.0 18.1 %all-gather.6.cloned.1.call-done = bf16[512,7168]{1,0:T(8,128)(2,1)} async-done(((bf16[512,3584]{1,0:T(8,128)(2,1)}), bf16[512,7168]{1,0:T(8,128)(2,1)}) %all-gather.6.cloned.1.call-update) | async-done | bytes 7340048 | tf_op jit(solution)/shard_map/all_gather | solution.py:40
  476.1 14.1 %fusion.41 = f32[512,1024]{1,0:T(8,128)} fusion(bf16[512,7168]{1,0:T(8,128)(2,1)} %all-gather.6.cloned.1.call-done, bf16[7168,1024]{1,0:T(8,128)(2,1)} %param.9), kind=kOutput, calls=%fused_computation.64 | convolution fusion | flops 7516192768 | bytes 24117248 | tf_op jit(solution)/shard_map/dot_general | solution.py:41
  490.2 0.0 all-gather.8.cloned.1.call-start
  490.3 36.5 %reduce-scatter.16.cloned.1.call-done = f32[128,1024]{1,0:T(8,128)} async-done(((f32[512,1024]{1,0:T(8,128)}), f32[128,1024]{1,0:T(8,128)}) %reduce-scatter.16.cloned.1.call-update) | async-done | bytes 524304 | tf_op jit(solution)/shard_map/reduce_scatter | solution.py:42
  526.7 1.9 subtract_convert_fusion
  528.7 26.7 %all-gather.8.cloned.1.call-done = bf16[512,1024]{1,0:T(8,128)(2,1)} async-done(((bf16[128,1024]{1,0:T(8,128)(2,1)}), bf16[512,1024]{1,0:T(8,128)(2,1)}) %all-gather.8.cloned.1.call-update) | async-done | bytes 1048592 | tf_op jit(solution)/shard_map/all_gather | solution.py:45
  555.4 14.4 %fusion.42 = f32[512,7168]{0,1:T(8,128)} fusion(bf16[512,1024]{1,0:T(8,128)(2,1)} %all-gather.8.cloned.1.call-done, bf16[7168,1024]{1,0:T(8,128)(2,1)} %param.9), kind=kOutput, calls=%fused_computation.65 | convolution fusion | flops 7516192768 | bytes 30408704 | tf_op jit(solution)/shard_map/dot_general | solution.py:49
  569.8 14.3 %copy.15 = f32[512,2,3584]{2,0,1:T(8,128)} copy(f32[512,2,3584]{0,2,1:T(8,128)} %bitcast.60) | data formatting | bytes 29360128 | tf_op jit(solution)/shard_map/reshape | solution.py:28
  584.1 0.0 reduce-scatter.20.cloned.1.call-start
  584.2 24.1 %reduce-scatter.18.cloned.1.call-done = f32[512,1,3584]{2,0,1:T(8,128)} async-done(((f32[512,2,3584]{2,0,1:T(8,128)}), f32[512,1,3584]{2,0,1:T(8,128)}) %reduce-scatter.18.cloned.1.call-update) | async-done | bytes 7340048 | tf_op jit(solution)/shard_map/reduce_scatter | solution.py:27
  608.3 5.3 convert_bitcast_fusion
  613.6 0.0 all-reduce.4.cloned.1.call-start
  613.7 0.8 copy-done.1
  614.5 1.7 fusion.23
  616.2 1.7 fusion.17
  617.9 1.7 fusion.21
  619.6 0.7 pad_maximum_fusion.1
  620.4 0.0 all-reduce.6.cloned.1.call-start
  620.4 62.9 %reduce-scatter.20.cloned.1.call-done = bf16[128,3584]{1,0:T(8,128)(2,1)} async-done(((bf16[512,3584]{1,0:T(8,128)(2,1)}), bf16[128,3584]{1,0:T(8,128)(2,1)}) %reduce-scatter.20.cloned.1.call-update) | async-done | bytes 917520 | tf_op jit(solution)/shard_map/reduce_scatter | solution.py:30
  683.3 3.0 fusion.15
  686.3 1.8 fusion.13
  688.1 0.7 pad_maximum_fusion.2
  688.7 52.3 %all-reduce.4.cloned.1.call-done = f32[512,128]{0,1:T(8,128)} async-done(((f32[512,128]{0,1:T(8,128)}), f32[512,128]{0,1:T(8,128)}) %all-reduce.4.cloned.1.call-update) | async-done | bytes 262160 | tf_op jit(solution)/shard_map/psum | solution.py:47
  741.1 0.8 constant_dynamic-slice_fusion
  741.8 52.7 %all-reduce.6.cloned.1.call-done = f32[128,192]{0,1:T(8,128)} async-done(((f32[128,192]{0,1:T(8,128)}), f32[128,192]{0,1:T(8,128)}) %all-reduce.6.cloned.1.call-update) | async-done | bytes 98320 | tf_op jit(solution)/shard_map/psum | solution.py:62
  794.5 0.8 slice.50
  795.2 1.0 convolution_bitcast_fusion.1
  796.3 1.0 convolution_bitcast_fusion.2
  797.3 1.0 convolution_bitcast_fusion
  798.4 0.9 reshape.33
  799.2 23.6 %all-reduce.7 = bf16[4,12288]{1,0:T(4,128)(2,1)S(1)} all-reduce(f32[4,12288]{1,0:T(4,128)} %reshape.33), channel_id=1, replica_groups=mesh['z'=4,'core'=2,'tensor'=4] {'z'}, use_global_device_ids=true, to_apply=%region_9.10 | all-reduce | flops 49152 | bytes 294912 | tf_op jit(solution)/shard_map/psum | solution.py:71
  822.9 1.5 fusion.43
  (28 shorter events, 0.4 us)
Async XLA Ops:
  6.5 816.3 %copy-start = (bf16[128,12288]{1,0:T(8,128)(2,1)S(1)}, bf16[128,12288]{1,0:T(8,128)(2,1)}, u32[]{:S(2)}) copy-start(bf16[128,12288]{1,0:T(8,128)(2,1)} %param.13) | copy-start | bytes 9437188
  6.5 205.9 %reduce-scatter.12.cloned.1.call-start = ((), (), s32[]{:S(2)}) async-start(), calls=%async_computation.9 | async-start | bytes 22020096 | tf_op jit(solution)/shard_map/reduce_scatter | solution.py:27
  136.7 102.5 %reduce-scatter.8.cloned.1.call-start = ((), (), s32[]{:S(2)}) async-start(), calls=%async_computation.7 | async-start | bytes 22020096 | tf_op jit(solution)/shard_map/reduce_scatter | solution.py:27
  212.4 98.7 %reduce-scatter.14.cloned.1.call-start = ((), (), s32[]{:S(2)}) async-start(), calls=%async_computation.10 | async-start | bytes 4587520 | tf_op jit(solution)/shard_map/reduce_scatter | solution.py:30
  217.8 164.2 %reduce-scatter.10.cloned.1.call-start = ((), (), s32[]{:S(2)}) async-start(), calls=%async_computation.8 | async-start | bytes 4587520 | tf_op jit(solution)/shard_map/reduce_scatter | solution.py:30
  244.5 213.2 %all-gather.4.cloned.1.call-start = ((), (), s32[]{:S(2)}) async-start(), calls=%async_computation.11 | async-start | bytes 4587520 | tf_op jit(solution)/shard_map/all_gather | solution.py:39
  385.0 91.0 %all-gather.6.cloned.1.call-start = ((), (), s32[]{:S(2)}) async-start(), calls=%async_computation.12 | async-start | bytes 11010048 | tf_op jit(solution)/shard_map/all_gather | solution.py:40
  457.7 69.0 %reduce-scatter.16.cloned.1.call-start = ((), (), s32[]{:S(2)}) async-start(), calls=%async_computation.13 | async-start | bytes 2621440 | tf_op jit(solution)/shard_map/reduce_scatter | solution.py:42
  490.2 65.2 %all-gather.8.cloned.1.call-start = ((), (), s32[]{:S(2)}) async-start(), calls=%async_computation.14 | async-start | bytes 1310720 | tf_op jit(solution)/shard_map/all_gather | solution.py:45
  528.6 79.6 %reduce-scatter.18.cloned.1.call-start = ((), (), s32[]{:S(2)}) async-start(), calls=%async_computation.16 | async-start | bytes 22020096 | tf_op jit(solution)/shard_map/reduce_scatter | solution.py:27
  584.1 99.2 %reduce-scatter.20.cloned.1.call-start = ((), (), s32[]{:S(2)}) async-start(), calls=%async_computation.17 | async-start | bytes 4587520 | tf_op jit(solution)/shard_map/reduce_scatter | solution.py:30
  613.6 0.9 copy-start.1
  613.6 127.5 %all-reduce.4.cloned.1.call-start = ((), (), s32[]{:S(2)}) async-start(), calls=%async_computation.15 | async-start | bytes 524288 | tf_op jit(solution)/shard_map/psum | solution.py:47
  620.4 174.1 %all-reduce.6.cloned.1.call-start = ((), (), s32[]{:S(2)}) async-start(), calls=%async_computation.18 | async-start | bytes 196608 | tf_op jit(solution)/shard_map/psum | solution.py:62
  683.3 3.0 copy-start.2
  683.3 3.0 copy-start.3
Sparse Core Ops, SparseCore 0:
  136.8 26.6 reduce-scatter.11
  212.5 26.6 reduce-scatter.7
  241.5 69.5 reduce-scatter.13
  313.3 68.7 reduce-scatter.9
  385.2 72.4 all-gather.3
  459.1 16.9 all-gather.5
  490.3 36.3 reduce-scatter.15
  528.7 26.6 all-gather.7
  584.2 23.9 reduce-scatter.17
  613.7 69.5 reduce-scatter.19
  685.7 55.2 all-reduce.3
  744.0 50.4 all-reduce.5
where the time goes:
time: 836 us; the launch traced here: 831 us
  waiting for transfers between devices  505 us (60%)
  local copies, waits for them, and re-layouts  195 us (23%)
  matrix products  71.6 us (9%)
  blocking collectives  23.6 us (3%)
  other arithmetic  22.2 us (3%)
  between operations  13.7 us (2%)
    reduce_scatter x3, waiting for transfers between devices, over_dp(): lax.psum_scatter(part.astype(jnp.bfloat16), 'z', scatter_dimension=0, til...  200 us
    all_gather x1, waiting for transfers between devices, local(): hidden = lax.all_gather(hidden_loc, 'z', axis=0, tiled=True)  72.6 us
    dot_general x1, local copies, waits for them, and re-layouts, local(): jnp.dot(tokens, w_gate_up[:, 0, :], preferred_element_type=jnp.float32)  61.2 us
    dot_general x1, local copies, waits for them, and re-layouts, local(): jnp.dot(tokens, w_gate_up[:, 1, :], preferred_element_type=jnp.float32)  60 us
    slice x1, local copies, waits for them, and re-layouts, local(): w_gate_up[:, 0, :]  55.9 us
    psum x1, waiting for transfers between devices, local(): b_sum = lax.psum(b_part, ('core', 'tensor'))  52.7 us
    psum x1, waiting for transfers between devices, local(): lax.psum(jnp.concatenate([a_in_part, a_out_part], axis=1), ('z', 'core'))  52.3 us
    reduce_scatter x3, waiting for transfers between devices, over_dp(): lax.psum_scatter(part.reshape(total, n_core, width_h), 'core', scatter_di...  45.5 us
  transfers between devices with their start and end apart: 12, of which 11 were waited for; matrix products, arithmetic and copies ran while one was open for 12% of the time, Pallas kernels for 0%

commit v1 on v0

--- a/solution.py
+++ b/solution.py
@@ -42,7 +42,14 @@
     out_rows = lax.psum_scatter(out_part, "tensor", scatter_dimension=0, tiled=True)
     tgt_rows = lax.dynamic_slice_in_dim(targets, t_idx * rows_t, rows_t, 0)
     cot_rows = (out_rows - tgt_rows.astype(jnp.float32)).astype(jnp.bfloat16)
-    cot = lax.all_gather(cot_rows, "tensor", axis=0, tiled=True)
+    ways, here = (lax.axis_size("tensor"), lax.axis_index("tensor"))
+    cot, reach = (cot_rows, 1)
+    while reach < ways:
+        theirs = lax.ppermute(cot, "tensor", [(d, d ^ reach) for d in range(ways)])
+        mine_first = jnp.concatenate([cot, theirs], axis=0)
+        theirs_first = jnp.concatenate([theirs, cot], axis=0)
+        cot = jnp.where(here & reach == 0, mine_first, theirs_first)
+        reach = 2 * reach
     a_out_part = jnp.dot(cot, proj_model[:, RANK:], preferred_element_type=jnp.float32)
     side = lax.psum(jnp.concatenate([a_in_part, a_out_part], axis=1), ("z", "core"))
     dh = over_dp(

time: 836 us -> 834 us (level)
  waiting for transfers between devices: 505 us -> 496 us
    all_gather x1 -> x0, waiting for transfers between devices: 26.7 us -> none  [local(): cot = lax.all_gather(cot_rows, 'tensor', axis=0, tiled=True)]
    ppermute x0 -> x2, waiting for transfers between devices: none -> 18.4 us  [local(): theirs = lax.ppermute(cot, 'tensor', [(d, d ^ reach) for d in range(ways)])]
  transfers between devices with their start and end apart: 12 -> 13, of which waited for: 11 -> 12; matrix products, arithmetic and copies ran while one was open for 12% -> 12% of each run, Pallas kernels for 0% -> 0%
where the time goes in v1:
time: 834 us; the launch traced here: 829 us
  waiting for transfers between devices  496 us (59%)
  local copies, waits for them, and re-layouts  195 us (23%)
  matrix products  74.4 us (9%)
  blocking collectives  23.6 us (3%)
  other arithmetic  23.5 us (3%)
  between operations  13.4 us (2%)
    reduce_scatter x3, waiting for transfers between devices, over_dp(): lax.psum_scatter(part.astype(jnp.bfloat16), 'z', scatter_dimension=0, til...  200 us
    all_gather x1, waiting for transfers between devices, local(): hidden = lax.all_gather(hidden_loc, 'z', axis=0, tiled=True)  72.6 us
    dot_general x1, local copies, waits for them, and re-layouts, local(): jnp.dot(tokens, w_gate_up[:, 0, :], preferred_element_type=jnp.float32)  61.2 us
    dot_general x1, local copies, waits for them, and re-layouts, local(): jnp.dot(tokens, w_gate_up[:, 1, :], preferred_element_type=jnp.float32)  60 us
    slice x1, local copies, waits for them, and re-layouts, local(): w_gate_up[:, 0, :]  55.9 us
    psum x1, waiting for transfers between devices, local(): b_sum = lax.psum(b_part, ('core', 'tensor'))  52.8 us
    psum x1, waiting for transfers between devices, local(): lax.psum(jnp.concatenate([a_in_part, a_out_part], axis=1), ('z', 'core'))  52.2 us
    reduce_scatter x3, waiting for transfers between devices, over_dp(): lax.psum_scatter(part.reshape(total, n_core, width_h), 'core', scatter_di...  45.5 us
  transfers between devices with their start and end apart: 13, of which 12 were waited for; matrix products, arithmetic and copies ran while one was open for 12% of the time, Pallas kernels for 0%

profile of v1, /device:TPU:0, one launch (start us, length us, event | category | flops | bytes accessed | tf_op | source)
XLA Modules:
  0.0 829.3 jit_solution(7546818917156869686)
XLA Ops:
  6.5 55.9 %fusion.43 = (bf16[1024,1,7168]{2,1,0:T(2,128)(2,1)}, bf16[1024,1,7168]{2,1,0:T(2,128)(2,1)}) fusion(bf16[1024,2,7168]{2,1,0:T(2,128)(2,1)} %param.8), kind=kLoop, calls=%fused_computation.68 | loop fusion | bytes 58720256 | tf_op jit(solution)/shard_map/slice | solution.py:34
  62.5 60.0 %copy.21 = bf16[1024,1,7168]{0,2,1:T(8,128)(2,1)} copy(bf16[1024,1,7168]{2,1,0:T(2,128)(2,1)} %get-tuple-element.6) | data formatting | bytes 29360128 | tf_op jit(solution)/shard_map/dot_general | solution.py:35
  122.5 14.3 %fusion.9 = f32[512,2,3584]{2,0,1:T(8,128)} fusion(bf16[2,3584,1024]{2,1,0:T(8,128)(2,1)} %bitcast.56, bf16[512,1024]{1,0:T(8,128)(2,1)} %param.7), kind=kOutput, calls=%fused_computation.22 | convolution fusion | flops 7516192768 | bytes 30408704 | tf_op jit(solution)/shard_map/dot_general | solution.py:35
  136.8 0.0 reduce-scatter.8.cloned.1.call-start
  136.9 61.2 %copy.20 = bf16[1024,1,7168]{0,2,1:T(8,128)(2,1)} copy(bf16[1024,1,7168]{2,1,0:T(2,128)(2,1)} %get-tuple-element.5) | data formatting | bytes 29360128 | tf_op jit(solution)/shard_map/dot_general | solution.py:34
  198.1 14.3 %fusion.11 = f32[512,2,3584]{2,0,1:T(8,128)} fusion(bf16[2,3584,1024]{2,1,0:T(8,128)(2,1)} %bitcast.57, bf16[512,1024]{1,0:T(8,128)(2,1)} %param.7), kind=kOutput, calls=%fused_computation.24 | convolution fusion | flops 7516192768 | bytes 30408704 | tf_op jit(solution)/shard_map/dot_general | solution.py:34
  212.5 5.4 convert_bitcast_fusion.1
  217.9 0.0 reduce-scatter.10.cloned.1.call-start
  218.0 21.3 %reduce-scatter.8.cloned.1.call-done = f32[512,1,3584]{2,0,1:T(8,128)} async-done(((f32[512,2,3584]{2,0,1:T(8,128)}), f32[512,1,3584]{2,0,1:T(8,128)}) %reduce-scatter.8.cloned.1.call-update) | async-done | bytes 7340048 | tf_op jit(solution)/shard_map/reduce_scatter | solution.py:27
  239.3 5.3 convert_bitcast_fusion.2
  244.7 66.6 %reduce-scatter.14.cloned.1.call-done = bf16[128,3584]{1,0:T(8,128)(2,1)} async-done(((bf16[512,3584]{1,0:T(8,128)(2,1)}), bf16[128,3584]{1,0:T(8,128)(2,1)}) %reduce-scatter.14.cloned.1.call-update) | async-done | bytes 917520 | tf_op jit(solution)/shard_map/reduce_scatter | solution.py:30
  311.2 71.0 %reduce-scatter.10.cloned.1.call-done = bf16[128,3584]{1,0:T(8,128)(2,1)} async-done(((bf16[512,3584]{1,0:T(8,128)(2,1)}), bf16[128,3584]{1,0:T(8,128)(2,1)}) %reduce-scatter.10.cloned.1.call-update) | async-done | bytes 917520 | tf_op jit(solution)/shard_map/reduce_scatter | solution.py:30
  382.2 2.9 fusion
  385.2 72.6 %all-gather.3.cloned.1.call-done = bf16[512,3584]{1,0:T(8,128)(2,1)} async-done(((bf16[128,3584]{1,0:T(8,128)(2,1)}), bf16[512,3584]{1,0:T(8,128)(2,1)}) %all-gather.3.cloned.1.call-update) | async-done | bytes 3670032 | tf_op jit(solution)/shard_map/all_gather | solution.py:39
  457.8 0.2 reduce-scatter.16.cloned.1.call-start
  458.0 18.1 %all-gather.5.cloned.1.call-done = bf16[512,7168]{1,0:T(8,128)(2,1)} async-done(((bf16[512,3584]{1,0:T(8,128)(2,1)}), bf16[512,7168]{1,0:T(8,128)(2,1)}) %all-gather.5.cloned.1.call-update) | async-done | bytes 7340048 | tf_op jit(solution)/shard_map/all_gather | solution.py:40
  476.1 14.1 %fusion.44 = f32[512,1024]{1,0:T(8,128)} fusion(bf16[512,7168]{1,0:T(8,128)(2,1)} %all-gather.5.cloned.1.call-done, bf16[7168,1024]{1,0:T(8,128)(2,1)} %param.9), kind=kOutput, calls=%fused_computation.69 | convolution fusion | flops 7516192768 | bytes 24117248 | tf_op jit(solution)/shard_map/dot_general | solution.py:41
  490.3 36.5 %reduce-scatter.16.cloned.1.call-done = f32[128,1024]{1,0:T(8,128)} async-done(((f32[512,1024]{1,0:T(8,128)}), f32[128,1024]{1,0:T(8,128)}) %reduce-scatter.16.cloned.1.call-update) | async-done | bytes 524304 | tf_op jit(solution)/shard_map/reduce_scatter | solution.py:42
  526.8 1.2 subtract_convert_fusion
  528.0 1.5 collective-permute-start
  529.5 6.7 collective-permute-done
  536.2 2.0 maximum_select_fusion.1
  538.2 1.4 collective-permute-start.1
  539.7 11.7 %collective-permute-done.1 = bf16[256,1024]{1,0:T(8,128)(2,1)} collective-permute-done((bf16[256,1024]{1,0:T(8,128)(2,1)}, bf16[256,1024]{1,0:T(8,128)(2,1)}, u32[]{:S(2)}, u32[]{:S(2)}) %collective-permute-start.1) | collective-permute-done | bytes 524320 | tf_op jit(solution)/shard_map/ppermute | solution.py:48
  551.3 16.8 %fusion.27 = f32[512,7168]{0,1:T(8,128)} fusion(bf16[7168,1024]{1,0:T(8,128)(2,1)} %param.9, bf16[256,1024]{1,0:T(8,128)(2,1)} %collective-permute-done.1, bf16[256,1024]{1,0:T(8,128)(2,1)} %maximum_select_fusion.1, pred[]{:T(512)S(6)} %eq.19), kind=kOutput, calls=%fused_computation.42 | convolution fusion | flops 7520911360 | bytes 30408704 | tf_op jit(solution)/shard_map/dot_general | solution.py:56
  568.1 14.3 %copy.15 = f32[512,2,3584]{2,0,1:T(8,128)} copy(f32[512,2,3584]{0,2,1:T(8,128)} %bitcast.58) | data formatting | bytes 29360128 | tf_op jit(solution)/shard_map/reshape | solution.py:28
  582.5 0.0 reduce-scatter.20.cloned.1.call-start
  582.5 24.1 %reduce-scatter.18.cloned.1.call-done = f32[512,1,3584]{2,0,1:T(8,128)} async-done(((f32[512,2,3584]{2,0,1:T(8,128)}), f32[512,1,3584]{2,0,1:T(8,128)}) %reduce-scatter.18.cloned.1.call-update) | async-done | bytes 7340048 | tf_op jit(solution)/shard_map/reduce_scatter | solution.py:27
  606.7 5.3 convert_bitcast_fusion
  612.1 0.8 copy-done.2
  612.9 1.7 fusion.23
  614.6 1.7 fusion.17
  616.3 2.1 fusion.21
  618.4 0.7 pad_maximum_fusion.1
  619.2 62.5 %reduce-scatter.20.cloned.1.call-done = bf16[128,3584]{1,0:T(8,128)(2,1)} async-done(((bf16[512,3584]{1,0:T(8,128)(2,1)}), bf16[128,3584]{1,0:T(8,128)(2,1)}) %reduce-scatter.20.cloned.1.call-update) | async-done | bytes 917520 | tf_op jit(solution)/shard_map/reduce_scatter | solution.py:30
  681.7 3.0 fusion.15
  684.7 1.8 fusion.13
  686.4 0.7 pad_maximum_fusion.2
  687.1 52.2 %all-reduce.4.cloned.1.call-done = f32[512,128]{0,1:T(8,128)} async-done(((f32[512,128]{0,1:T(8,128)}), f32[512,128]{0,1:T(8,128)}) %all-reduce.4.cloned.1.call-update) | async-done | bytes 262160 | tf_op jit(solution)/shard_map/psum | solution.py:54
  739.3 0.8 constant_dynamic-slice_fusion
  740.1 52.8 %all-reduce.6.cloned.1.call-done = f32[128,192]{0,1:T(8,128)} async-done(((f32[128,192]{0,1:T(8,128)}), f32[128,192]{0,1:T(8,128)}) %all-reduce.6.cloned.1.call-update) | async-done | bytes 98320 | tf_op jit(solution)/shard_map/psum | solution.py:69
  792.9 0.8 slice.50
  793.7 1.0 convolution_bitcast_fusion.1
  794.7 1.0 convolution_bitcast_fusion.2
  795.7 1.0 convolution_bitcast_fusion
  796.8 0.9 reshape.33
  797.7 23.6 %all-reduce.7 = bf16[4,12288]{1,0:T(4,128)(2,1)S(1)} all-reduce(f32[4,12288]{1,0:T(4,128)} %reshape.33), channel_id=1, replica_groups=mesh['z'=4,'core'=2,'tensor'=4] {'z'}, use_global_device_ids=true, to_apply=%region_9.10 | all-reduce | flops 49152 | bytes 294912 | tf_op jit(solution)/shard_map/psum | solution.py:78
  821.3 1.5 fusion.45
  (30 shorter events, 0.5 us)
Async XLA Ops:
  6.5 814.7 %copy-start = (bf16[128,12288]{1,0:T(8,128)(2,1)S(1)}, bf16[128,12288]{1,0:T(8,128)(2,1)}, u32[]{:S(2)}) copy-start(bf16[128,12288]{1,0:T(8,128)(2,1)} %param.13) | copy-start | bytes 9437188
  6.5 206.0 %reduce-scatter.12.cloned.1.call-start = ((), (), s32[]{:S(2)}) async-start(), calls=%async_computation.9 | async-start | bytes 22020096 | tf_op jit(solution)/shard_map/reduce_scatter | solution.py:27
  136.8 102.5 %reduce-scatter.8.cloned.1.call-start = ((), (), s32[]{:S(2)}) async-start(), calls=%async_computation.7 | async-start | bytes 22020096 | tf_op jit(solution)/shard_map/reduce_scatter | solution.py:27
  212.4 98.8 %reduce-scatter.14.cloned.1.call-start = ((), (), s32[]{:S(2)}) async-start(), calls=%async_computation.10 | async-start | bytes 4587520 | tf_op jit(solution)/shard_map/reduce_scatter | solution.py:30
  217.9 164.3 %reduce-scatter.10.cloned.1.call-start = ((), (), s32[]{:S(2)}) async-start(), calls=%async_computation.8 | async-start | bytes 4587520 | tf_op jit(solution)/shard_map/reduce_scatter | solution.py:30
  244.6 213.2 %all-gather.3.cloned.1.call-start = ((), (), s32[]{:S(2)}) async-start(), calls=%async_computation.11 | async-start | bytes 4587520 | tf_op jit(solution)/shard_map/all_gather | solution.py:39
  385.1 91.0 %all-gather.5.cloned.1.call-start = ((), (), s32[]{:S(2)}) async-start(), calls=%async_computation.12 | async-start | bytes 11010048 | tf_op jit(solution)/shard_map/all_gather | solution.py:40
  457.8 69.0 %reduce-scatter.16.cloned.1.call-start = ((), (), s32[]{:S(2)}) async-start(), calls=%async_computation.13 | async-start | bytes 2621440 | tf_op jit(solution)/shard_map/reduce_scatter | solution.py:42
  490.3 116.4 %reduce-scatter.18.cloned.1.call-start = ((), (), s32[]{:S(2)}) async-start(), calls=%async_computation.15 | async-start | bytes 22020096 | tf_op jit(solution)/shard_map/reduce_scatter | solution.py:27
  528.0 8.2 collective-permute-start
  538.2 13.1 %collective-permute-start.1 = (bf16[256,1024]{1,0:T(8,128)(2,1)}, bf16[256,1024]{1,0:T(8,128)(2,1)}, u32[]{:S(2)}, u32[]{:S(2)}) collective-permute-start(bf16[256,1024]{1,0:T(8,128)(2,1)} %maximum_select_fusion.1), channel_id=1, source_target_pairs={{0,2},{1,3},{2,0},{3,1},{4,6},{5,7},{6,4},{7,5},{8,10},{9,11},{10,... | collective-permute-start | bytes 1572872 | tf_op jit(solution)/shard_map/ppermute | solution.py:48
  582.5 99.2 %reduce-scatter.20.cloned.1.call-start = ((), (), s32[]{:S(2)}) async-start(), calls=%async_computation.16 | async-start | bytes 4587520 | tf_op jit(solution)/shard_map/reduce_scatter | solution.py:30
  611.9 0.9 copy-start.2
  612.0 127.4 %all-reduce.4.cloned.1.call-start = ((), (), s32[]{:S(2)}) async-start(), calls=%async_computation.14 | async-start | bytes 524288 | tf_op jit(solution)/shard_map/psum | solution.py:54
  619.1 173.8 %all-reduce.6.cloned.1.call-start = ((), (), s32[]{:S(2)}) async-start(), calls=%async_computation.17 | async-start | bytes 196608 | tf_op jit(solution)/shard_map/psum | solution.py:69
  681.7 3.0 copy-start.1
  681.7 3.0 copy-start.3
Sparse Core Ops, SparseCore 0:
  137.0 26.6 reduce-scatter.11
  212.6 26.6 reduce-scatter.7
  241.6 69.5 reduce-scatter.13
  313.4 68.7 reduce-scatter.9
  385.2 72.4 all-gather.2
  459.2 16.9 all-gather.4
  490.4 36.3 reduce-scatter.15
  582.6 23.9 reduce-scatter.17
  612.1 69.5 reduce-scatter.19
  684.0 55.3 all-reduce.3
  742.4 50.4 all-reduce.5
